TPU v7x, 128 devices: a whole 4x4x4 slice. The times are simulated.
128 devices in a mesh: req: 16 (over z, x), exp: 8 (over y, core).
Axes of the slice: x: 4, y: 4, z: 4, core: 2. Of those that a mesh axis runs over, the one named last changes fastest.
Arguments:
- tokens: bfloat16 [12288, 2880], P(('req', 'exp')), may hold values from -6 to 6
- attn_gain: float32 [2880], replicated, may hold values from 0.5 to 8
- w_query: bfloat16 [2880, 4096], P(None, 'exp'), may hold values from -0.109375 to 0.109375
- key_weight: bfloat16 [2880, 512], P(None, 'exp'), may hold values from -0.109375 to 0.109375
- value_weight: bfloat16 [2880, 512], P(None, 'exp'), may hold values from -0.109375 to 0.109375
- sinks: float32 [64], P('exp'), may hold values from -1 to 3
- w_out: bfloat16 [4096, 2880], P('exp'), may hold values from -0.09375 to 0.09375
- ffn_gain: float32 [2880], replicated, may hold values from 0.25 to 1.75
- router: bfloat16 [2880, 32], replicated, may hold values from -0.109375 to 0.109375
- routes: int32 [12288, 4], P(('req', 'exp')), may hold values from 0 to 31, all different within a row; in each aligned block of 96 rows (0 to 95, 96 to 191, ...) at most 14 rows name the same one
- lengths: int32 [16, 6], P('req'), may hold values from 1 to 384, 768 in all within a row
- expert_gate: bfloat16 [128, 2880, 720], P(('req', 'exp')), may hold values from -0.109375 to 0.109375
- expert_up: bfloat16 [128, 2880, 720], P(('req', 'exp')), may hold values from -0.109375 to 0.109375
- expert_down: bfloat16 [128, 720, 2880], P(('req', 'exp')), may hold values from -0.109375 to 0.109375
Outputs:
- layer_out: bfloat16 [12288, 2880], P(('req', 'exp'))
Inputs may be any that keep to these rules, and one draw needn't show every extreme that they name: `routes`: in the rows of one device no expert is named by more than 14 rows, a bound that some block reaches; a row names 4 different experts.
All inputs are finite; a program needn't handle non-finite values.
Results may differ from a plain program's by a relative error of at most 0.02.
The roundings to bfloat16 on the way count: a program that leaves them out, or rounds other values in their place, can miss the bound.
Values may be sent and summed in bfloat16 or wider, within the bound.
No kernel may reach another device: no remote copies, remote signals or barrier semaphores. Data moves between devices by JAX's collectives and lax.ppermute only.
A program may use at most 192 MiB of HBM per device.

v0:
```python
import jax
import jax.numpy as jnp
from jax import lax
from jax.sharding import PartitionSpec as P

QUERY_HEADS = 64
KEY_VALUE_HEADS = 8
HEAD_DIM = 64
EXPERTS = 32
TOPK = 4
CAP = 14


def rms_norm(value_rows, gain):
    mean_sq = jnp.mean(value_rows * value_rows, axis=-1, keepdims=True)
    return value_rows * lax.rsqrt(mean_sq + 1e-05) * gain


def rotate(value_rows, offset):
    half = value_rows.shape[-1] // 2
    freqs = jnp.exp(
        -(2.0 * jnp.arange(half, dtype=jnp.float32) / value_rows.shape[-1])
        * jnp.log(jnp.float32(150000.0))
    )
    angle = offset.astype(jnp.float32)[:, None] * freqs[None, :]
    cosine = jnp.cos(angle)[:, None, :]
    sine = jnp.sin(angle)[:, None, :]
    first = value_rows[..., :half]
    second = value_rows[..., half:]
    return jnp.concatenate(
        [first * cosine - second * sine, second * cosine + first * sine], axis=-1
    )


def per_device(
    tokens,
    attn_gain,
    w_query,
    key_weight,
    value_weight,
    sinks,
    w_out,
    ffn_gain,
    router,
    routes,
    lengths,
    expert_gate,
    expert_up,
    expert_down,
):
    tok_rows = tokens.shape[0]
    model_width = tokens.shape[1]
    local_heads = w_query.shape[1] // HEAD_DIM
    local_kv = key_weight.shape[1] // HEAD_DIM
    head_group = QUERY_HEADS // KEY_VALUE_HEADS
    normed_input = rms_norm(tokens.astype(jnp.float32), attn_gain).astype(jnp.bfloat16)
    piece = lax.all_gather(normed_input, "exp", axis=0, tiled=True)
    projected = jnp.concatenate(
        [
            jnp.dot(piece, w_query, preferred_element_type=jnp.float32),
            jnp.dot(piece, key_weight, preferred_element_type=jnp.float32),
            jnp.dot(piece, value_weight, preferred_element_type=jnp.float32),
        ],
        axis=1,
    )
    item_count = projected.shape[0]
    lens = lengths[0]
    ends = jnp.cumsum(lens)
    starts = ends - lens
    position = jnp.arange(item_count, dtype=jnp.int32)
    member = ((position[:, None] >= starts[None, :]) & (position[:, None] < ends[None, :])).astype(
        jnp.int32
    )
    segment = jnp.sum(member * jnp.arange(lens.shape[0], dtype=jnp.int32)[None, :], axis=1)
    offset = position - jnp.sum(member * starts[None, :], axis=1)
    q_width = local_heads * HEAD_DIM
    kv_width = local_kv * HEAD_DIM
    query_rows = rotate(
        projected[:, :q_width].reshape(item_count, local_heads, HEAD_DIM), offset
    ).astype(jnp.bfloat16)
    key_rows = rotate(
        projected[:, q_width : q_width + kv_width].reshape(item_count, local_kv, HEAD_DIM), offset
    ).astype(jnp.bfloat16)
    value_rows = (
        projected[:, q_width + kv_width :]
        .reshape(item_count, local_kv, HEAD_DIM)
        .astype(jnp.bfloat16)
    )
    grouped_heads = query_rows.reshape(item_count, local_kv, head_group, HEAD_DIM)
    scores = jnp.einsum(
        "qcgd,kcd->cgqk", grouped_heads, key_rows, preferred_element_type=jnp.float32
    ) * HEAD_DIM ** (-0.5)
    allowed = (segment[:, None] == segment[None, :]) & (position[None, :] <= position[:, None])
    sink_score_logit = sinks.reshape(local_kv, head_group, 1, 1)
    masked = jnp.where(allowed[None, None], scores, -jnp.inf)
    top = jnp.maximum(jnp.max(masked, axis=-1, keepdims=True), sink_score_logit)
    expo = jnp.where(allowed[None, None], jnp.exp(scores - top), 0.0)
    denom = jnp.sum(expo, axis=-1, keepdims=True) + jnp.exp(sink_score_logit - top)
    probs = (expo / denom).astype(jnp.bfloat16)
    attended = jnp.einsum("cgqk,kcd->qcgd", probs, value_rows, preferred_element_type=jnp.float32)
    attended = attended.reshape(item_count, q_width).astype(jnp.bfloat16)
    attn_sum = lax.psum_scatter(
        jnp.dot(attended, w_out, preferred_element_type=jnp.float32).astype(jnp.bfloat16),
        "exp",
        scatter_dimension=0,
        tiled=True,
    ).astype(jnp.float32)
    residual = (tokens.astype(jnp.float32) + attn_sum).astype(jnp.bfloat16)
    normed2 = rms_norm(residual.astype(jnp.float32), ffn_gain).astype(jnp.bfloat16)
    logits = jnp.dot(normed2, router, preferred_element_type=jnp.float32)
    picked = jnp.take_along_axis(logits, routes, axis=1)
    weights = jax.nn.softmax(picked, axis=-1)
    flat_routes = routes.reshape(-1)
    expert_ids = jnp.arange(EXPERTS, dtype=jnp.int32)
    onehot_route = (flat_routes[:, None] == expert_ids[None, :]).astype(jnp.int32)
    rank = jnp.cumsum(onehot_route, axis=0) - 1
    slot_rank = jnp.sum(onehot_route * rank, axis=1)
    flat_slot = flat_routes * CAP + slot_rank
    slot_ids = jnp.arange(EXPERTS * CAP, dtype=jnp.int32)
    dispatch_table = (slot_ids[:, None] == flat_slot[None, :]).astype(jnp.bfloat16)
    repeated = jnp.repeat(normed2, TOPK, axis=0)
    packed = jnp.dot(dispatch_table, repeated, preferred_element_type=jnp.float32).astype(
        jnp.bfloat16
    )
    n_req = lax.axis_size("req")
    n_exp = lax.axis_size("exp")
    devices = n_req * n_exp
    split = devices // EXPERTS
    send_rows = jnp.broadcast_to(
        packed.reshape(EXPERTS, 1, CAP, model_width), (EXPERTS, split, CAP, model_width)
    ).reshape(devices, CAP, model_width)
    received = lax.all_to_all(send_rows, ("req", "exp"), split_axis=0, concat_axis=0, tiled=True)
    flat_rows = received.reshape(-1, model_width)
    gate = jnp.dot(flat_rows, expert_gate[0], preferred_element_type=jnp.float32)
    up_val = jnp.dot(flat_rows, expert_up[0], preferred_element_type=jnp.float32)
    hidden = ((up_val + 1.0) * gate * jax.nn.sigmoid(1.702 * gate)).astype(jnp.bfloat16)
    slice_out = jnp.dot(hidden, expert_down[0], preferred_element_type=jnp.float32).astype(
        jnp.bfloat16
    )
    returned = lax.all_to_all(
        slice_out.reshape(received.shape), ("req", "exp"), split_axis=0, concat_axis=0, tiled=True
    )
    summed = returned.astype(jnp.float32).reshape(EXPERTS, split, CAP, model_width).sum(axis=1)
    summed = summed.reshape(EXPERTS * CAP, model_width)
    picked_rows = jnp.take(summed, flat_slot, axis=0).reshape(tok_rows, TOPK, model_width)
    moe_sum = jnp.sum(weights[:, :, None] * picked_rows, axis=1)
    return (residual.astype(jnp.float32) + moe_sum).astype(jnp.bfloat16)


def solution(mesh):
    return jax.shard_map(
        per_device,
        mesh=mesh,
        in_specs=(
            P(("req", "exp"), None),
            P(),
            P(None, "exp"),
            P(None, "exp"),
            P(None, "exp"),
            P("exp"),
            P("exp", None),
            P(),
            P(),
            P(("req", "exp"), None),
            P("req", None),
            P(("req", "exp"), None, None),
            P(("req", "exp"), None, None),
            P(("req", "exp"), None, None),
        ),
        out_specs=P(("req", "exp"), None),
        check_vma=False,
    )
```

profile of v0, /device:TPU:14, one launch (start us, length us, event | category | flops | bytes accessed | tf_op | source)
XLA Modules:
  0.0 587.9 jit_solution(4064006883043466249)
XLA Ops:
  6.5 1.4 fusion.19
  8.0 2.1 fusion.21
  10.0 0.0 all-gather.2.cloned.1.call-update
  10.1 0.0 reduce-scatter.2.cloned.1.call-start
  10.1 0.8 reduce-window.10
  11.0 0.7 fusion.52
  11.6 0.1 select_reduce_fusion.1
  11.7 1.1 multiply_cosine_fusion
  12.8 0.4 fusion.13
  13.2 31.8 %all-gather.2.cloned.1.call-done = bf16[768,2880]{1,0:T(8,128)(2,1)} async-done(((bf16[96,2880]{1,0:T(8,128)(2,1)}), bf16[768,2880]{1,0:T(8,128)(2,1)}) %all-gather.2.cloned.1.call-update) | async-done | bytes 4423696 | tf_op jit(solution)/shard_map/all_gather | solution.py:57
  45.0 3.9 convolution_bitcast_fusion
  48.9 0.4 fusion.46
  49.4 4.6 fusion.59
  54.0 0.2 subtract_convert_fusion
  54.2 0.0 copy-start.11
  54.2 8.6 %fusion = (f32[8,768]{1,0:T(8,128)S(1)}, f32[768,768,8]{1,0,2:T(8,128)}) fusion(pred[768,768]{0,1:T(8,128)(4,1)S(1)} %fusion.13, bf16[768,8,32]{0,2,1:T(8,128)(2,1)S(1)} %get-tuple-element.10, bf16[768,8,32]{0,2,1:T(8,128)(2,1)S(1)} %get-tuple-element.9, bf16[768,32]{0,1:T(8,128)(2,1)S(1)} %get-tuple-element.12, bf16[768,32]{0,1:T(8,128)(2,1)S(1)} %get-tuple-element.11), kind=kOutput, calls=%fused_computation.5 | convolution fusion | flops 619898880 | bytes 20373504 | tf_op jit(solution)/shard_map/qcgd,kcd->cgqk/dot_general | solution.py:90
  62.9 0.6 copy-done.7
  63.5 0.7 broadcast_maximum_fusion
  64.2 10.8 %fusion.3 = f32[8,768]{1,0:T(8,128)} fusion(f32[768,768,8]{1,0,2:T(8,128)} %get-tuple-element.16, f32[8,768]{1,0:T(8,128)} %broadcast_maximum_fusion, pred[768,768]{0,1:T(8,128)(4,1)S(1)} %fusion.13), kind=kLoop, calls=%fused_computation.9 | loop fusion | flops 18868224 | bytes 19513344 | tf_op jit(solution)/shard_map/reduce_sum | solution.py:98
  75.0 1.4 exponential_add_fusion
  76.4 14.1 %fusion.16 = bf16[64,8,768]{2,0,1:T(8,128)(2,1)} fusion(f32[8,768]{1,0:T(8,128)} %exponential_add_fusion, f32[8,768]{1,0:T(8,128)} %broadcast_maximum_fusion, f32[768,768,8]{1,0,2:T(8,128)} %get-tuple-element.16, pred[768,768]{0,1:T(8,128)(4,1)S(1)} %fusion.13, bf16[768,2880]{1,0:T(8,128)(2,1)} %all-gather.2.cloned.1.call-done, bf16[2880,64]{0,1:T(8,128)(2,1)} %param.18), kind=kOutput, calls=%fused_computation.30 | convolution fusion | flops 911130624 | bytes 25092096 | tf_op jit(solution)/shard_map/cgqk,kcd->qcgd/dot_general | solution.py:100
  90.5 5.8 convolution_convert_fusion.1
  96.3 0.0 reduce-scatter.2.cloned.1.call-update
  96.3 0.7 copy-done.9
  97.0 0.1 copy.44
  97.1 0.1 reshape.415
  97.2 0.1 eq.59
  97.3 1.0 reduce-window.11
  98.4 0.2 slice_reduce_fusion
  98.6 0.1 fusion.44
  98.7 33.6 %reduce-scatter.2.cloned.1.call-done = bf16[96,2880]{1,0:T(8,128)(2,1)} async-done(((bf16[768,2880]{1,0:T(8,128)(2,1)}), bf16[96,2880]{1,0:T(8,128)(2,1)}) %reduce-scatter.2.cloned.1.call-update) | async-done | bytes 552976 | tf_op jit(solution)/shard_map/reduce_scatter | solution.py:102
  132.4 1.3 fusion.23
  133.7 1.3 fusion.25
  135.0 0.6 broadcast_in_dim.40
  135.6 2.4 reshape.417
  138.1 4.7 convolution_convert_fusion.2
  142.8 4.4 broadcast_in_dim.41
  147.2 7.1 %broadcast_in_dim.42 = bf16[32,4,14,2880]{3,2,1,0:T(8,128)(2,1)} broadcast(bf16[32,14,2880]{2,1,0:T(8,128)(2,1)} %broadcast_in_dim.41), dimensions={0,2,3} | broadcast | bytes 12902400 | tf_op jit(solution)/shard_map/broadcast_in_dim | solution.py:129
  154.3 146.0 %all_to_all.10 = bf16[128,14,2880]{2,1,0:T(8,128)(2,1)} all-to-all(bf16[128,14,2880]{2,1,0:T(8,128)(2,1)} %bitcast.104), channel_id=1, replica_groups=mesh['req'=16,'exp'=8] {'req','exp'}, dimensions={0} | all-to-all | bytes 20643840 | tf_op jit(solution)/shard_map/all_to_all | solution.py:132
  300.4 15.4 %reshape.419 = bf16[1792,2880]{1,0:T(8,128)(2,1)} reshape(bf16[128,14,2880]{2,1,0:T(8,128)(2,1)} %all_to_all.10) | data formatting | bytes 20643840 | tf_op jit(solution)/shard_map/reshape | solution.py:133
  315.7 14.6 %fusion.7 = f32[1792,720]{0,1:T(8,128)} fusion(bf16[1792,2880]{1,0:T(8,128)(2,1)} %reshape.419, bf16[1,2880,720]{1,2,0:T(8,128)(2,1)} %param.25), kind=kOutput, calls=%fused_computation.18 | convolution fusion | flops 7431782400 | bytes 19630080 | tf_op jit(solution)/shard_map/dot_general | solution.py:134
  330.3 27.2 %convolution_convert_fusion = bf16[1792,2880]{0,1:T(8,128)(2,1)} fusion(bf16[1,720,2880]{2,1,0:T(8,128)(2,1)} %param.27, f32[1792,720]{0,1:T(8,128)} %fusion.7, bf16[1792,2880]{1,0:T(8,128)(2,1)} %reshape.419, bf16[1,2880,720]{1,2,0:T(8,128)(2,1)} %param.26), kind=kOutput, calls=%fused_computation.10 | convolution fusion | flops 14879047680 | bytes 34099200 | tf_op jit(solution)/shard_map/dot_general | solution.py:137
  357.6 14.3 %copy.49 = bf16[1792,2880]{1,0:T(8,128)(2,1)} copy(bf16[1792,2880]{0,1:T(8,128)(2,1)} %convolution_convert_fusion) | data formatting | bytes 20643840 | tf_op jit(solution)/shard_map/convert_element_type | solution.py:137
  371.9 14.4 %reshape.420 = bf16[128,14,2880]{2,1,0:T(8,128)(2,1)} reshape(bf16[1792,2880]{1,0:T(8,128)(2,1)} %copy.49) | data formatting | bytes 20643840 | tf_op jit(solution)/shard_map/reshape | solution.py:141
  386.3 8.2 %all-to-all-start.1 = ((bf16[128,14,2880]{2,1,0:T(8,128)(2,1)}), bf16[128,14,2880]{2,1,0:T(8,128)(2,1)}, u32[]{:S(2)}, u32[]{:S(2)}) async-start(bf16[128,14,2880]{2,1,0:T(8,128)(2,1)} %reshape.420), calls=%async_computation.2 | async-start | bytes 24117248 | tf_op jit(solution)/shard_map/all_to_all | solution.py:140
  394.5 0.1 reduce_sum.92
  394.7 0.1 copy.50
  394.8 0.1 mul.250
  394.9 0.1 copy.41
  395.0 0.1 reshape.434
  395.1 0.1 copy.47
  395.2 0.1 copy.48
  395.4 0.3 fusion.60
  395.7 2.9 gather_fusion.1
  398.6 0.1 reshape.437
  398.7 0.1 copy.42
  398.8 0.7 copy.43
  399.5 143.8 %all-to-all-done.1 = bf16[128,14,2880]{2,1,0:T(8,128)(2,1)} async-done(((bf16[128,14,2880]{2,1,0:T(8,128)(2,1)}), bf16[128,14,2880]{2,1,0:T(8,128)(2,1)}, u32[]{:S(2)}, u32[]{:S(2)}) %all-to-all-start.1) | async-done | bytes 10321952 | tf_op jit(solution)/shard_map/all_to_all | solution.py:140
  543.3 9.8 %convert_reduce_fusion = f32[32,14,2880]{2,1,0:T(8,128)} fusion(bf16[128,14,2880]{2,1,0:T(8,128)(2,1)} %all-to-all-done.1), kind=kLoop, calls=%fused_computation.2 | loop fusion | flops 9031680 | bytes 15482880 | tf_op jit(solution)/shard_map/reduce_sum | solution.py:143
  553.1 5.6 reshape.423
  558.7 9.1 %gather_fusion = f32[384,2880]{1,0:T(8,128)} fusion(f32[448,2880]{1,0:T(8,128)} %reshape.423, s32[1024]{0:T(1024)S(1)} %pad_clamp_fusion), kind=kCustom, calls=%fused_computation | custom fusion | bytes 8848896 | tf_op jit(solution)/shard_map/jit(_take)/gather | solution.py:145
  567.8 5.5 gather.12
  573.3 6.5 %multiply_reduce_fusion = f32[96,2880]{1,0:T(8,128)S(1)} fusion(f32[96,4,2880]{2,1,0:T(4,128)} %gather.12, f32[96,4]{1,0:T(8,128)} %copy.43, pred[96,4]{1,0:T(8,128)(4,1)S(1)} %copy.48), kind=kLoop, calls=%fused_computation.15 | loop fusion | flops 3041280 | bytes 5531520 | tf_op jit(solution)/shard_map/reduce_sum | solution.py:146
  579.9 1.0 fusion.26
  (37 shorter events, 0.2 us)
Async XLA Ops:
  6.5 83.9 %copy-start = (bf16[512,2880]{0,1:T(8,128)(2,1)S(1)}, bf16[512,2880]{0,1:T(8,128)(2,1)}, u32[]{:S(2)}) copy-start(bf16[512,2880]{0,1:T(8,128)(2,1)} %param.20) | copy-start | bytes 8847364
  6.5 38.4 %all-gather.2.cloned.1.call-start = ((), (), s32[]{:S(2)}) async-start(), calls=%async_computation.3 | async-start | bytes 5087232 | tf_op jit(solution)/shard_map/all_gather | solution.py:57
  10.1 122.3 %reduce-scatter.2.cloned.1.call-start = ((), (), s32[]{:S(2)}) async-start(), calls=%async_computation.4 | async-start | bytes 5087232 | tf_op jit(solution)/shard_map/reduce_scatter | solution.py:102
  45.0 4.4 copy-start.4
  49.3 4.7 copy-start.5
  49.3 4.7 copy-start.6
  54.2 9.3 %copy-start.11 = (f32[8]{0:T(128)S(1)}, f32[8]{0:T(128)}, u32[]{:S(2)}) copy-start(f32[8]{0:T(128)} %param.19) | copy-start | bytes 100
  62.9 0.6 copy-start.7
  96.3 0.7 copy-start.9
  96.3 36.1 %copy-start.2 = (bf16[96,2880]{1,0:T(8,128)(2,1)S(1)}, bf16[96,2880]{1,0:T(8,128)(2,1)}, u32[]{:S(2)}) copy-start(bf16[96,2880]{1,0:T(8,128)(2,1)} %param.14) | copy-start | bytes 1658884
  96.3 37.4 %copy-start.10 = (f32[2880]{0:T(1024)S(1)}, f32[2880]{0:T(1024)}, u32[]{:S(2)}) copy-start(f32[2880]{0:T(1024)} %param.21) | copy-start | bytes 34564
  386.3 9.0 %copy-start.8 = (bf16[2880,32]{0,1:T(8,128)(2,1)S(1)}, bf16[2880,32]{0,1:T(8,128)(2,1)}, u32[]{:S(2)}) copy-start(bf16[2880,32]{0,1:T(8,128)(2,1)} %param.22) | copy-start | bytes 552964
  386.3 157.0 %all-to-all-start.1 = ((bf16[128,14,2880]{2,1,0:T(8,128)(2,1)}), bf16[128,14,2880]{2,1,0:T(8,128)(2,1)}, u32[]{:S(2)}, u32[]{:S(2)}) async-start(bf16[128,14,2880]{2,1,0:T(8,128)(2,1)} %reshape.420), calls=%async_computation.2 | async-start | bytes 24117248 | tf_op jit(solution)/shard_map/all_to_all | solution.py:140
  567.8 13.1 %copy-start.1 = (bf16[512,2880]{0,1:T(8,128)(2,1)S(1)}, bf16[512,2880]{0,1:T(8,128)(2,1)}, u32[]{:S(2)}) copy-start(bf16[512,2880]{0,1:T(8,128)(2,1)} %param.20) | copy-start | bytes 8847364
  573.3 6.5 %copy-start.3 = (bf16[96,2880]{1,0:T(8,128)(2,1)S(1)}, bf16[96,2880]{1,0:T(8,128)(2,1)}, u32[]{:S(2)}) copy-start(bf16[96,2880]{1,0:T(8,128)(2,1)} %reduce-scatter.2.cloned.1.call-done) | copy-start | bytes 1658884
Sparse Core Ops, SparseCore 0:
  10.2 34.7 all-gather.1
  96.5 35.8 reduce-scatter.1
where the time goes:
time: 594 us; the launch traced here: 588 us
  waiting for transfers between devices  209 us (35%)
  blocking collectives  146 us (25%)
  local copies, waits for them, and re-layouts  85.3 us (14%)
  matrix products  83.9 us (14%)
  other arithmetic  41.3 us (7%)
  between operations  13.9 us (2%)
  starting transfers between devices  8.24 us (1%)
    all_to_all x1, blocking collectives, per_device(): lax.all_to_all(send_rows, ('req', 'exp'), split_axis=0, concat_axis=0, ti...  146 us
    all_to_all x1, waiting for transfers between devices, per_device(): lax.all_to_all(slice_out.reshape(received.shape), ('req', 'exp'), split_a...  144 us
    reduce_scatter x1, waiting for transfers between devices, per_device(): lax.psum_scatter(jnp.dot(attended, w_out, preferred_element_type=jnp.floa...  33.6 us
    all_gather x1, waiting for transfers between devices, per_device(): piece = lax.all_gather(normed_input, 'exp', axis=0, tiled=True)  31.8 us
    dot_general x1, matrix products, per_device(): jnp.dot(hidden, expert_down[0], preferred_element_type=jnp.float32)  27.2 us
    reshape x1, local copies, waits for them, and re-layouts, per_device(): flat_rows = received.reshape(-1, model_width)  15.4 us
    gather x2, local copies, waits for them, and re-layouts, per_device(): jnp.take(summed, flat_slot, axis=0).reshape(tok_rows, TOPK, model_width)  14.6 us
    dot_general x1, matrix products, per_device(): jnp.dot(flat_rows, expert_gate[0], preferred_element_type=jnp.float32)  14.6 us
  transfers between devices with their start and end apart: 3, of which 3 were waited for; matrix products, arithmetic and copies ran while one was open for 2% of the time, Pallas kernels for 0%

commit v1 on v0

--- a/solution.py
+++ b/solution.py
@@ -54,7 +54,9 @@
     local_kv = key_weight.shape[1] // HEAD_DIM
     head_group = QUERY_HEADS // KEY_VALUE_HEADS
     normed_input = rms_norm(tokens.astype(jnp.float32), attn_gain).astype(jnp.bfloat16)
-    piece = lax.all_gather(normed_input, "exp", axis=0, tiled=True)
+    piece = jnp.concatenate(
+        lax.all_to_all(jnp.stack([normed_input] * lax.axis_size("exp")), "exp", 0, 0), axis=0
+    )
     projected = jnp.concatenate(
         [
             jnp.dot(piece, w_query, preferred_element_type=jnp.float32),

time: 594 us -> 622 us (1.047)
  waiting for transfers between devices: 209 us -> 223 us
  local copies, waits for them, and re-layouts: 85.3 us -> 92.3 us
    all_to_all x0 -> x1, waiting for transfers between devices: none -> 45.5 us  [per_device(): lax.all_to_all(jnp.stack([normed_input] * lax.axis_size('exp')), 'exp', 0...]
    all_gather x1 -> x0, waiting for transfers between devices: 31.8 us -> none  [per_device(): piece = lax.all_gather(normed_input, 'exp', axis=0, tiled=True)]
where the time goes in v1:
time: 622 us; the launch traced here: 612 us
  waiting for transfers between devices  223 us (36%)
  blocking collectives  146 us (23%)
  local copies, waits for them, and re-layouts  92.3 us (15%)
  matrix products  84.2 us (14%)
  other arithmetic  39 us (6%)
  between operations  13.9 us (2%)
  starting transfers between devices  13.1 us (2%)
    all_to_all x1, blocking collectives, per_device(): lax.all_to_all(send_rows, ('req', 'exp'), split_axis=0, concat_axis=0, ti...  146 us
    all_to_all x1, waiting for transfers between devices, per_device(): lax.all_to_all(slice_out.reshape(received.shape), ('req', 'exp'), split_a...  144 us
    all_to_all x1, waiting for transfers between devices, per_device(): lax.all_to_all(jnp.stack([normed_input] * lax.axis_size('exp')), 'exp', 0...  45.5 us
    reduce_scatter x1, waiting for transfers between devices, per_device(): lax.psum_scatter(jnp.dot(attended, w_out, preferred_element_type=jnp.floa...  34.2 us
    dot_general x1, matrix products, per_device(): jnp.dot(hidden, expert_down[0], preferred_element_type=jnp.float32)  27.2 us
    reshape x1, local copies, waits for them, and re-layouts, per_device(): flat_rows = received.reshape(-1, model_width)  15.4 us
    gather x2, local copies, waits for them, and re-layouts, per_device(): jnp.take(summed, flat_slot, axis=0).reshape(tok_rows, TOPK, model_width)  14.6 us
    dot_general x1, matrix products, per_device(): jnp.dot(flat_rows, expert_gate[0], preferred_element_type=jnp.float32)  14.6 us
  transfers between devices with their start and end apart: 3, of which 3 were waited for; matrix products, arithmetic and copies ran while one was open for 2% of the time, Pallas kernels for 0%

profile of v1, /device:TPU:14, one launch (start us, length us, event | category | flops | bytes accessed | tf_op | source)
XLA Modules:
  0.0 612.2 jit_solution(966165134406298358)
XLA Ops:
  6.5 1.4 fusion.19
  8.0 1.3 fusion.21
  9.2 2.4 stack.2
  11.6 4.9 all-to-all-start
  16.5 4.6 copy.46
  21.1 0.2 reduce-window.10
  21.3 0.1 select_reduce_fusion.1
  21.4 1.1 multiply_cosine_fusion
  22.5 0.4 fusion.13
  22.9 45.5 %all-to-all-done = bf16[8,96,2880]{2,1,0:T(8,128)(2,1)} async-done(((bf16[8,96,2880]{2,1,0:T(8,128)(2,1)}), bf16[8,96,2880]{2,1,0:T(8,128)(2,1)}, u32[]{:S(2)}, u32[]{:S(2)}) %all-to-all-start) | async-done | bytes 4423712 | tf_op jit(solution)/shard_map/all_to_all | solution.py:58
  68.4 3.9 convolution_bitcast_fusion
  72.3 0.4 fusion.46
  72.7 0.0 copy-start.5
  72.8 5.0 fusion.59
  77.7 0.2 subtract_convert_fusion
  78.0 8.2 %fusion = (f32[8,768]{1,0:T(8,128)S(1)}, f32[768,768,8]{1,0,2:T(8,128)}) fusion(pred[768,768]{0,1:T(8,128)(4,1)S(1)} %fusion.13, bf16[768,8,32]{0,2,1:T(8,128)(2,1)S(1)} %get-tuple-element.10, bf16[768,8,32]{0,2,1:T(8,128)(2,1)S(1)} %get-tuple-element.9, bf16[768,32]{0,1:T(8,128)(2,1)S(1)} %get-tuple-element.12, bf16[768,32]{0,1:T(8,128)(2,1)S(1)} %get-tuple-element.11), kind=kOutput, calls=%fused_computation.5 | convolution fusion | flops 619898880 | bytes 20373504 | tf_op jit(solution)/shard_map/qcgd,kcd->cgqk/dot_general | solution.py:92
  86.2 0.6 copy-done.7
  86.8 0.7 broadcast_maximum_fusion
  87.4 10.8 %fusion.3 = f32[8,768]{1,0:T(8,128)} fusion(f32[768,768,8]{1,0,2:T(8,128)} %get-tuple-element.16, f32[8,768]{1,0:T(8,128)} %broadcast_maximum_fusion, pred[768,768]{0,1:T(8,128)(4,1)S(1)} %fusion.13), kind=kLoop, calls=%fused_computation.9 | loop fusion | flops 18868224 | bytes 19513344 | tf_op jit(solution)/shard_map/reduce_sum | solution.py:100
  98.2 1.4 exponential_add_fusion
  99.7 14.5 %fusion.16 = bf16[64,8,768]{2,0,1:T(8,128)(2,1)} fusion(f32[8,768]{1,0:T(8,128)} %exponential_add_fusion, f32[8,768]{1,0:T(8,128)} %broadcast_maximum_fusion, f32[768,768,8]{1,0,2:T(8,128)} %get-tuple-element.16, pred[768,768]{0,1:T(8,128)(4,1)S(1)} %fusion.13, bf16[768,2880]{1,0:T(8,128)(2,1)} %bitcast, bf16[2880,64]{0,1:T(8,128)(2,1)} %param.18), kind=kOutput, calls=%fused_computation.30 | convolution fusion | flops 911130624 | bytes 25092096 | tf_op jit(solution)/shard_map/cgqk,kcd->qcgd/dot_general | solution.py:102
  114.2 5.8 convolution_convert_fusion.1
  120.0 0.0 reduce-scatter.2.cloned.1.call-update
  120.1 0.7 copy-done.9
  120.7 0.1 copy.52
  120.8 0.1 eq.59
  120.9 0.1 reshape.419
  121.0 0.9 reduce-window.11
  121.9 0.2 slice_reduce_fusion
  122.2 0.1 fusion.44
  122.3 34.2 %reduce-scatter.2.cloned.1.call-done = bf16[96,2880]{1,0:T(8,128)(2,1)} async-done(((bf16[768,2880]{1,0:T(8,128)(2,1)}), bf16[96,2880]{1,0:T(8,128)(2,1)}) %reduce-scatter.2.cloned.1.call-update) | async-done | bytes 552976 | tf_op jit(solution)/shard_map/reduce_scatter | solution.py:104
  156.5 1.3 fusion.23
  157.9 1.3 fusion.25
  159.1 0.6 broadcast_in_dim.40
  159.7 2.4 reshape.421
  162.2 4.7 convolution_convert_fusion.2
  166.9 4.4 broadcast_in_dim.41
  171.3 7.1 %broadcast_in_dim.42 = bf16[32,4,14,2880]{3,2,1,0:T(8,128)(2,1)} broadcast(bf16[32,14,2880]{2,1,0:T(8,128)(2,1)} %broadcast_in_dim.41), dimensions={0,2,3} | broadcast | bytes 12902400 | tf_op jit(solution)/shard_map/broadcast_in_dim | solution.py:131
  178.4 146.2 %all_to_all.15 = bf16[128,14,2880]{2,1,0:T(8,128)(2,1)} all-to-all(bf16[128,14,2880]{2,1,0:T(8,128)(2,1)} %bitcast.109), channel_id=1, replica_groups=mesh['req'=16,'exp'=8] {'req','exp'}, dimensions={0} | all-to-all | bytes 20643840 | tf_op jit(solution)/shard_map/all_to_all | solution.py:134
  324.7 15.4 %reshape.423 = bf16[1792,2880]{1,0:T(8,128)(2,1)} reshape(bf16[128,14,2880]{2,1,0:T(8,128)(2,1)} %all_to_all.15) | data formatting | bytes 20643840 | tf_op jit(solution)/shard_map/reshape | solution.py:135
  340.0 14.6 %fusion.7 = f32[1792,720]{0,1:T(8,128)} fusion(bf16[1792,2880]{1,0:T(8,128)(2,1)} %reshape.423, bf16[1,2880,720]{1,2,0:T(8,128)(2,1)} %param.25), kind=kOutput, calls=%fused_computation.18 | convolution fusion | flops 7431782400 | bytes 19630080 | tf_op jit(solution)/shard_map/dot_general | solution.py:136
  354.6 27.2 %convolution_convert_fusion = bf16[1792,2880]{0,1:T(8,128)(2,1)} fusion(bf16[1,720,2880]{2,1,0:T(8,128)(2,1)} %param.27, f32[1792,720]{0,1:T(8,128)} %fusion.7, bf16[1792,2880]{1,0:T(8,128)(2,1)} %reshape.423, bf16[1,2880,720]{1,2,0:T(8,128)(2,1)} %param.26), kind=kOutput, calls=%fused_computation.10 | convolution fusion | flops 14879047680 | bytes 34099200 | tf_op jit(solution)/shard_map/dot_general | solution.py:139
  381.8 14.3 %copy.57 = bf16[1792,2880]{1,0:T(8,128)(2,1)} copy(bf16[1792,2880]{0,1:T(8,128)(2,1)} %convolution_convert_fusion) | data formatting | bytes 20643840 | tf_op jit(solution)/shard_map/convert_element_type | solution.py:139
  396.2 14.4 %reshape.424 = bf16[128,14,2880]{2,1,0:T(8,128)(2,1)} reshape(bf16[1792,2880]{1,0:T(8,128)(2,1)} %copy.57) | data formatting | bytes 20643840 | tf_op jit(solution)/shard_map/reshape | solution.py:143
  410.6 8.2 %all-to-all-start.2 = ((bf16[128,14,2880]{2,1,0:T(8,128)(2,1)}), bf16[128,14,2880]{2,1,0:T(8,128)(2,1)}, u32[]{:S(2)}, u32[]{:S(2)}) async-start(bf16[128,14,2880]{2,1,0:T(8,128)(2,1)} %reshape.424), calls=%async_computation.3 | async-start | bytes 24117248 | tf_op jit(solution)/shard_map/all_to_all | solution.py:142
  418.8 0.1 reduce_sum.92
  418.9 0.1 copy.49
  419.0 0.1 reshape.438
  419.1 0.1 copy.58
  419.3 0.1 mul.250
  419.4 0.1 copy.55
  419.5 0.1 copy.56
  419.6 0.3 fusion.60
  419.9 2.9 gather_fusion.1
  422.8 0.1 reshape.441
  422.9 0.1 copy.50
  423.1 0.7 copy.51
  423.8 143.8 %all-to-all-done.2 = bf16[128,14,2880]{2,1,0:T(8,128)(2,1)} async-done(((bf16[128,14,2880]{2,1,0:T(8,128)(2,1)}), bf16[128,14,2880]{2,1,0:T(8,128)(2,1)}, u32[]{:S(2)}, u32[]{:S(2)}) %all-to-all-start.2) | async-done | bytes 10321952 | tf_op jit(solution)/shard_map/all_to_all | solution.py:142
  567.6 9.8 %convert_reduce_fusion = f32[32,14,2880]{2,1,0:T(8,128)} fusion(bf16[128,14,2880]{2,1,0:T(8,128)(2,1)} %all-to-all-done.2), kind=kLoop, calls=%fused_computation.2 | loop fusion | flops 9031680 | bytes 15482880 | tf_op jit(solution)/shard_map/reduce_sum | solution.py:145
  577.4 5.6 reshape.427
  583.0 9.1 %gather_fusion = f32[384,2880]{1,0:T(8,128)} fusion(f32[448,2880]{1,0:T(8,128)} %reshape.427, s32[1024]{0:T(1024)S(1)} %pad_clamp_fusion), kind=kCustom, calls=%fused_computation | custom fusion | bytes 8848896 | tf_op jit(solution)/shard_map/jit(_take)/gather | solution.py:147
  592.1 5.5 gather.12
  597.6 6.5 %multiply_reduce_fusion = f32[96,2880]{1,0:T(8,128)S(1)} fusion(f32[96,4,2880]{2,1,0:T(4,128)} %gather.12, f32[96,4]{1,0:T(8,128)} %copy.51, pred[96,4]{1,0:T(8,128)(4,1)S(1)} %copy.56), kind=kLoop, calls=%fused_computation.15 | loop fusion | flops 3041280 | bytes 5531520 | tf_op jit(solution)/shard_map/reduce_sum | solution.py:148
  604.1 1.0 fusion.26
  (40 shorter events, 0.2 us)
Async XLA Ops:
  6.5 107.7 %copy-start = (bf16[512,2880]{0,1:T(8,128)(2,1)S(1)}, bf16[512,2880]{0,1:T(8,128)(2,1)}, u32[]{:S(2)}) copy-start(bf16[512,2880]{0,1:T(8,128)(2,1)} %param.20) | copy-start | bytes 8847364
  11.6 56.8 %all-to-all-start = ((bf16[8,96,2880]{2,1,0:T(8,128)(2,1)}), bf16[8,96,2880]{2,1,0:T(8,128)(2,1)}, u32[]{:S(2)}, u32[]{:S(2)}) async-start(bf16[8,96,2880]{2,1,0:T(8,128)(2,1)} %stack.2), calls=%async_computation | async-start | bytes 9043968 | tf_op jit(solution)/shard_map/all_to_all | solution.py:58
  16.5 4.6 copy-start.12
  16.5 140.0 %reduce-scatter.2.cloned.1.call-start = ((), (), s32[]{:S(2)}) async-start(), calls=%async_computation.4 | async-start | bytes 5087232 | tf_op jit(solution)/shard_map/reduce_scatter | solution.py:104
  68.4 4.4 copy-start.4
  72.7 5.0 copy-start.5
  72.7 5.0 copy-start.6
  78.0 8.8 %copy-start.11 = (f32[8]{0:T(128)S(1)}, f32[8]{0:T(128)}, u32[]{:S(2)}) copy-start(f32[8]{0:T(128)} %param.19) | copy-start | bytes 100
  86.2 0.6 copy-start.7
  120.0 0.7 copy-start.9
  120.0 36.5 %copy-start.2 = (bf16[96,2880]{1,0:T(8,128)(2,1)S(1)}, bf16[96,2880]{1,0:T(8,128)(2,1)}, u32[]{:S(2)}) copy-start(bf16[96,2880]{1,0:T(8,128)(2,1)} %param.14) | copy-start | bytes 1658884
  120.0 37.8 %copy-start.10 = (f32[2880]{0:T(1024)S(1)}, f32[2880]{0:T(1024)}, u32[]{:S(2)}) copy-start(f32[2880]{0:T(1024)} %param.21) | copy-start | bytes 34564
  410.6 9.0 %copy-start.8 = (bf16[2880,32]{0,1:T(8,128)(2,1)S(1)}, bf16[2880,32]{0,1:T(8,128)(2,1)}, u32[]{:S(2)}) copy-start(bf16[2880,32]{0,1:T(8,128)(2,1)} %param.22) | copy-start | bytes 552964
  410.6 157.0 %all-to-all-start.2 = ((bf16[128,14,2880]{2,1,0:T(8,128)(2,1)}), bf16[128,14,2880]{2,1,0:T(8,128)(2,1)}, u32[]{:S(2)}, u32[]{:S(2)}) async-start(bf16[128,14,2880]{2,1,0:T(8,128)(2,1)} %reshape.424), calls=%async_computation.3 | async-start | bytes 24117248 | tf_op jit(solution)/shard_map/all_to_all | solution.py:142
  592.1 13.1 %copy-start.1 = (bf16[512,2880]{0,1:T(8,128)(2,1)S(1)}, bf16[512,2880]{0,1:T(8,128)(2,1)}, u32[]{:S(2)}) copy-start(bf16[512,2880]{0,1:T(8,128)(2,1)} %param.20) | copy-start | bytes 8847364
  597.6 6.5 %copy-start.3 = (bf16[96,2880]{1,0:T(8,128)(2,1)S(1)}, bf16[96,2880]{1,0:T(8,128)(2,1)}, u32[]{:S(2)}) copy-start(bf16[96,2880]{1,0:T(8,128)(2,1)} %reduce-scatter.2.cloned.1.call-done) | copy-start | bytes 1658884
Sparse Core Ops, SparseCore 0:
  120.2 36.2 reduce-scatter.1
